TPU v7x, 32 devices: a whole 2x2x4 slice. The times are simulated.
32 devices in a mesh: tm: 8 (over z, y), cal: 4 (over x, core).
Axes of the slice: x: 2, y: 2, z: 4, core: 2. Of those that a mesh axis runs over, the one named last changes fastest.
Arguments:
- src_design: float32 [5, 4096, 128], P(None, ('tm', 'cal')), may hold values from -6 to 6
- att_design: float32 [3, 4096, 128], P(None, ('tm', 'cal')), may hold values from -6 to 6
- obs_phase: float32 [4096, 128], P(('tm', 'cal')), may hold values from 0 to 1
- cal_design: float32 [4096, 128], P(('tm', 'cal')), may hold values from -6 to 6
- obs_weight: float32 [4096, 128], P(('tm', 'cal')), may hold values from 0.1 to 12
- knot_index: int32 [4096, 128], P(('tm', 'cal')), may hold values from 0 to 4092, as said below
- cal_block: int32 [4096, 128], P(('tm', 'cal')), may hold values from 0 to 7
- cal_column: int32 [4096, 128], P(('tm', 'cal')), may hold values from 0 to 4095
- obs_count: int32 [4096], P(('tm', 'cal')), may hold values from 32 to 128
- src_res: float32 [5, 4096], P(None, ('tm', 'cal')), may hold values from -6 to 6
- att_res: float32 [3, 4096], P(None, ('tm', 'cal')), may hold values from -6 to 6
- cal_res: float32 [8, 4096], P('cal'), may hold values from -6 to 6
- src_dir: float32 [5, 4096], P(None, ('tm', 'cal')), may hold values from -6 to 6
- att_dir: float32 [3, 4096], P(None, ('tm', 'cal')), may hold values from -6 to 6
- cal_dir: float32 [8, 4096], P('cal'), may hold values from -6 to 6
Outputs:
- new_src_res: float32 [5, 4096], P(None, ('tm', 'cal'))
- new_att_res: float32 [3, 4096], P(None, ('tm', 'cal'))
- new_cal_res: float32 [8, 4096], P('cal')
- new_src_dir: float32 [5, 4096], P(None, ('tm', 'cal'))
- new_att_dir: float32 [3, 4096], P(None, ('tm', 'cal'))
- new_cal_dir: float32 [8, 4096], P('cal')
Inputs may be any that keep to these rules, and one draw needn't show every extreme that they name: The observations of source row s have knot intervals from (s // 128) * 128 to (s // 128) * 128 + 127, and knot_index + 3 < 4096.
All inputs are finite; a program needn't handle non-finite values.
Results may differ from a plain program's by a relative error of at most 0.00015.
Values sent between devices are 32-bit elements; how exact they have to be, the bound alone decides.
No kernel may reach another device: no remote copies, remote signals or barrier semaphores. Data moves between devices by JAX's collectives and lax.ppermute only.
A program may use at most 64 MiB of HBM per device.

v0:
```python
import jax
import jax.numpy as jnp
from jax import lax
from jax.sharding import PartitionSpec as P

EXACT = lax.Precision.HIGHEST


def passed_along(block, axis, distance):
    devices = range(lax.axis_size(axis))
    route = [(i - distance, i) for i in devices if i - distance in devices]
    return lax.ppermute(block, axis, route)


def spline(phase):
    rest = 1.0 - phase
    cube = phase * phase * phase
    square = phase * phase
    first = rest * rest * rest / 6.0
    second = (3.0 * cube - 6.0 * square + 4.0) / 6.0
    third = (-3.0 * cube + 3.0 * square + 3.0 * phase + 1.0) / 6.0
    fourth = cube / 6.0
    return (first, second, third, fourth)


def local(
    src_design,
    att_design,
    obs_phase,
    cal_design,
    obs_weight,
    knot_index,
    cal_block,
    cal_column,
    obs_count,
    src_res,
    att_res,
    cal_res,
    src_dir,
    att_dir,
    cal_dir,
):
    knot_count = att_dir.shape[1]
    blocks, col_width = cal_dir.shape
    all_blocks = blocks * lax.axis_size("cal")
    cal_size = all_blocks * col_width
    lane = 128
    rows = cal_size // lane
    src_rows, slots = obs_phase.shape
    first_row = (lax.axis_index("tm") == 0).astype(jnp.float32)
    cal_values = lax.all_gather(cal_dir, "cal", axis=0, tiled=True)
    edge_knots = passed_along(att_dir[:, :3], ("tm", "cal"), -1)
    att_ext = jnp.concatenate([att_dir, edge_knots], axis=1)
    live_mask = (lax.broadcasted_iota(jnp.int32, obs_phase.shape, 1) < obs_count[:, None]).astype(
        jnp.float32
    )
    basis = spline(obs_phase)
    local_knot = knot_index - lax.axis_index(("tm", "cal")) * knot_count
    knot_iota = lax.broadcasted_iota(jnp.int32, (knot_count, 1, 1), 0)
    knot_hot = (local_knot[None] == knot_iota).astype(jnp.float32)
    table = jnp.stack([att_ext[:, m : m + knot_count].T for m in range(4)], axis=1)
    table = table.reshape(knot_count, 12)
    picked = jnp.einsum("jq,jso->qso", table, knot_hot, precision=EXACT).reshape(
        4, 3, src_rows, slots
    )
    y_att = jnp.zeros_like(obs_phase)
    for m in range(4):
        y_att = y_att + basis[m] * jnp.sum(att_design * picked[m], axis=0)
    flat_index = cal_block * col_width + cal_column
    high = flat_index // lane
    low = flat_index % lane
    high_hot = (high[None] == lax.broadcasted_iota(jnp.int32, (rows, 1, 1), 0)).astype(jnp.float32)
    low_hot = (low[None] == lax.broadcasted_iota(jnp.int32, (lane, 1, 1), 0)).astype(jnp.float32)
    cal_table = cal_values.reshape(rows, lane)
    row_vals = jnp.einsum("hl,hso->lso", cal_table, high_hot, precision=EXACT)
    y_cal = cal_design * jnp.sum(row_vals * low_hot, axis=0)
    y_src = jnp.sum(src_design * src_dir[:, :, None], axis=0)
    response = live_mask * (y_src + y_att + y_cal)
    weighted = obs_weight * response
    curv_local = jnp.sum(weighted * response)
    norm_local = (
        jnp.sum(src_res * src_res)
        + jnp.sum(att_res * att_res)
        + first_row * jnp.sum(cal_res * cal_res)
    )
    q_src = jnp.sum(src_design * weighted[None], axis=2)
    scaled = att_design * weighted[None]
    spread = jnp.stack([basis[m][None] * scaled for m in range(4)], axis=0).reshape(
        12, src_rows, slots
    )
    gathered = jnp.einsum("qso,jso->jq", spread, knot_hot, precision=EXACT).reshape(
        knot_count, 4, 3
    )
    grad_ext = jnp.zeros((3, knot_count + 3), jnp.float32)
    for m in range(4):
        grad_ext = grad_ext + jnp.pad(gathered[:, m, :].T, ((0, 0), (m, 3 - m)))
    incoming = passed_along(grad_ext[:, knot_count:], ("tm", "cal"), 1)
    q_att = jnp.concatenate([grad_ext[:, :3] + incoming, grad_ext[:, 3:knot_count]], axis=1)
    cal_weighted = (cal_design * weighted)[None] * low_hot
    cal_term = jnp.einsum("hso,lso->hl", high_hot, cal_weighted, precision=EXACT)
    scalars = jnp.zeros((1, lane), jnp.float32).at[0, 0].set(norm_local).at[0, 1].set(curv_local)
    packed = jnp.concatenate([cal_term, scalars], axis=0)
    summed = lax.psum(packed, ("tm", "cal"))
    norm_now = summed[rows, 0]
    curvature = summed[rows, 1]
    own = lax.axis_index("cal") * (blocks * col_width // lane)
    q_cal = lax.dynamic_slice_in_dim(summed, own, blocks * col_width // lane, 0).reshape(
        blocks, col_width
    )
    step_len = norm_now / curvature
    new_src_res = src_res - step_len * q_src
    new_att_res = att_res - step_len * q_att
    new_cal_res = cal_res - step_len * q_cal
    next_local = (
        jnp.sum(new_src_res * new_src_res)
        + jnp.sum(new_att_res * new_att_res)
        + first_row * jnp.sum(new_cal_res * new_cal_res)
    )
    norm_next = lax.psum(jnp.zeros((1, lane), jnp.float32).at[0, 0].set(next_local), ("tm", "cal"))[
        0, 0
    ]
    ratio = norm_next / norm_now
    return (
        new_src_res,
        new_att_res,
        new_cal_res,
        new_src_res + ratio * src_dir,
        new_att_res + ratio * att_dir,
        new_cal_res + ratio * cal_dir,
    )


def solution(mesh):
    return jax.shard_map(
        local,
        mesh=mesh,
        in_specs=(
            P(None, ("tm", "cal"), None),
            P(None, ("tm", "cal"), None),
            P(("tm", "cal"), None),
            P(("tm", "cal"), None),
            P(("tm", "cal"), None),
            P(("tm", "cal"), None),
            P(("tm", "cal"), None),
            P(("tm", "cal"), None),
            P(("tm", "cal")),
            P(None, ("tm", "cal")),
            P(None, ("tm", "cal")),
            P("cal", None),
            P(None, ("tm", "cal")),
            P(None, ("tm", "cal")),
            P("cal", None),
        ),
        out_specs=(
            P(None, ("tm", "cal")),
            P(None, ("tm", "cal")),
            P("cal", None),
            P(None, ("tm", "cal")),
            P(None, ("tm", "cal")),
            P("cal", None),
        ),
        check_vma=False,
    )
```

profile of v0, /device:TPU:0, one launch (start us, length us, event | category | flops | bytes accessed | tf_op | source)
XLA Modules:
  0.0 323.5 jit_solution(16515309153429786869)
XLA Ops:
  7.2 1.3 collective-permute-start
  10.5 1.4 multiply_reduce_fusion.4
  11.9 1.3 multiply_reduce_fusion.8
  13.2 1.3 multiply_reduce_fusion.6
  17.7 0.8 broadcast_subtract_fusion
  18.6 7.7 %all-gather = f32[4,2,4096]{2,1,0:T(2,128)S(1)} all-gather(f32[1,2,4096]{2,1,0:T(2,128)} %bitcast.78), channel_id=1, replica_groups=mesh['tm'=8,'cal'=4] {'cal'}, dimensions={0}, use_global_device_ids=true | all-gather | bytes 163840 | tf_op jit(solution)/shard_map/all_gather | solution.py:51
  26.4 0.9 add_select_fusion.1
  27.4 1.3 iota_compare_fusion.1
  28.7 38.5 %copy.50 = pred[128,128,128]{2,0,1:T(32,128)(4,1)S(1)} copy(pred[128,128,128]{1,0,2:T(32,128)(4,1)S(1)} %iota_compare_fusion.1) | data formatting | bytes 4194304 | tf_op jit(solution)/shard_map/eq | solution.py:60
  67.2 2.7 iota_compare_fusion
  70.0 20.5 %copy.55 = pred[256,128,128]{2,0,1:T(32,128)(4,1)} copy(pred[256,128,128]{1,0,2:T(32,128)(4,1)S(1)} %iota_compare_fusion) | data formatting | bytes 8388608 | tf_op jit(solution)/shard_map/eq | solution.py:72
  90.7 8.2 %fusion = f32[128,128]{1,0:T(8,128)S(1)} fusion(s32[128,128]{1,0:T(8,128)S(1)} %get-tuple-element.62, pred[256,128,128]{2,0,1:T(32,128)(4,1)} %copy.55, f32[256,128]{1,0:T(8,128)S(1)} %reshape.140), kind=kOutput, calls=%fused_computation.2 | convolution fusion | flops 6448726016 | bytes 4456448 | tf_op jit(solution)/shard_map/hl,hso->lso/dot_general | solution.py:75
  99.1 2.2 fusion.29
  101.3 0.8 fusion.7
  102.9 4.2 %fusion.4 = f32[128,4,3]{0,1,2:T(4,128)S(1)} fusion(f32[4,3,128,128]{3,0,2,1:T(4,128)S(1)} %copy.59, s32[128,128]{0,1:T(8,128)S(1)} %copy.49), kind=kOutput, calls=%fused_computation.9 | convolution fusion | flops 304087040 | bytes 858112 | tf_op jit(solution)/shard_map/qso,jso->jq/dot_general | solution.py:91
  107.9 2.2 collective-permute-start.1
  110.1 4.7 %fusion.1 = f32[128,128,128]{2,0,1:T(8,128)} fusion(f32[128,128]{1,0:T(8,128)S(1)} %get-tuple-element.52, s32[128,128]{1,0:T(8,128)S(1)} %get-tuple-element.62), kind=kLoop, calls=%fused_computation.5 | loop fusion | flops 4194304 | bytes 8519680 | tf_op jit(solution)/shard_map/mul | solution.py:99
  114.8 9.3 %copy.57 = f32[128,128,128]{1,0,2:T(8,128)} copy(f32[128,128,128]{2,0,1:T(8,128)} %fusion.1) | data formatting | bytes 16777216 | tf_op jit(solution)/shard_map/mul | solution.py:99
  124.2 11.2 %convolution_bitcast_fusion = f32[256,128]{1,0:T(8,128)S(1)} fusion(f32[128,128,128]{1,0,2:T(8,128)} %copy.57, s32[128,128]{0,1:T(8,128)S(1)} %copy.48), kind=kOutput, calls=%fused_computation.8 | convolution fusion | flops 6446645248 | bytes 8585216 | tf_op jit(solution)/shard_map/hso,lso->hl/dot_general | solution.py:100
  135.3 2.5 fusion.28
  137.9 1.4 scatter.11
  140.0 123.3 %all-reduce.8.cloned.1.call-done = f32[257,128]{1,0:T(8,128)} async-done(((f32[257,128]{1,0:T(8,128)}), f32[257,128]{1,0:T(8,128)}) %all-reduce.8.cloned.1.call-update) | async-done | bytes 131600 | tf_op jit(solution)/shard_map/psum | solution.py:103
  263.3 1.3 fusion.26
  271.6 42.5 %psum.15 = f32[1,128]{1,0:T(1,128)S(1)} all-reduce(f32[1,128]{1,0:T(1,128)S(1)} %scatter.14), channel_id=1, replica_groups=mesh['tm'=8,'cal'=4] {'tm','cal'}, use_global_device_ids=true, to_apply=%region_17.18 | all-reduce | flops 128 | bytes 1024 | tf_op jit(solution)/shard_map/psum | solution.py:119
  (71 shorter events, 10.1 us)
Async XLA Ops:
  7.2 256.2 %all-reduce.8.cloned.1.call-start = ((), (), s32[]{:S(2)}) async-start(), calls=%async_computation | async-start | bytes 270336 | tf_op jit(solution)/shard_map/psum | solution.py:103
  7.2 91.8 %collective-permute-start = (f32[3,3]{1,0:T(4,128)}, f32[3,3]{1,0:T(4,128)S(1)}, u32[]{:S(2)}, u32[]{:S(2)}) collective-permute-start(f32[3,3]{1,0:T(4,128)} %bitcast.79), channel_id=1, source_target_pairs={{1,0},{2,1},{3,2},{4,3},{5,4},{6,5},{7,6},{8,7},{9,8},{10,9},{11,1... | collective-permute-start | bytes 116 | tf_op jit(solution)/shard_map/ppermute | solution.py:12
  69.9 20.6 %copy-start = (f32[5,128,128]{2,1,0:T(8,128)S(1)}, f32[5,128,128]{2,1,0:T(8,128)}, u32[]{:S(2)}) copy-start(f32[5,128,128]{2,1,0:T(8,128)} %param.21) | copy-start | bytes 983044
  69.9 20.6 %copy-start.9 = (f32[5,128]{1,0:T(8,128)S(1)}, f32[5,128]{1,0:T(8,128)}, u32[]{:S(2)}) copy-start(f32[5,128]{1,0:T(8,128)} %param.33) | copy-start | bytes 7684
  90.7 8.4 %copy-start.8 = (f32[3,128]{1,0:T(4,128)S(1)}, f32[3,128]{1,0:T(4,128)}, u32[]{:S(2)}) copy-start(f32[3,128]{1,0:T(4,128)} %param.34) | copy-start | bytes 4612
  90.7 10.6 %copy-start.1 = (f32[3,128,128]{2,1,0:T(8,128)S(1)}, f32[3,128,128]{2,1,0:T(8,128)}, u32[]{:S(2)}) copy-start(f32[3,128,128]{2,1,0:T(8,128)} %param.22) | copy-start | bytes 589828
  98.9 3.2 copy-start.5
  98.9 3.2 copy-start.6
  98.9 3.2 copy-start.7
  99.0 3.2 copy-start.14
  107.9 32.1 %collective-permute-start.1 = (f32[3,3]{1,0:T(4,128)S(1)}, f32[3,3]{1,0:T(4,128)S(1)}, u32[]{:S(2)}, u32[]{:S(2)}) collective-permute-start(f32[3,3]{1,0:T(4,128)S(1)} %slice.142), channel_id=1, source_target_pairs={{0,1},{1,2},{2,3},{3,4},{4,5},{5,6},{6,7},{7,8},{8,9},{9,10},{10,1... | collective-permute-start | bytes 116 | tf_op jit(solution)/shard_map/ppermute | solution.py:12
  124.2 142.6 %copy-start.11 = (f32[5,128]{1,0:T(8,128)S(1)}, f32[5,128]{1,0:T(8,128)}, u32[]{:S(2)}) copy-start(f32[5,128]{1,0:T(8,128)} %param.30) | copy-start | bytes 7684
  124.2 143.3 %copy-start.4 = (f32[2,4096]{1,0:T(2,128)S(1)}, f32[2,4096]{1,0:T(2,128)}, u32[]{:S(2)}) copy-start(f32[2,4096]{1,0:T(2,128)} %param.32) | copy-start | bytes 98308
  124.2 144.7 %copy-start.12 = (f32[3,128]{1,0:T(4,128)S(1)}, f32[3,128]{1,0:T(4,128)}, u32[]{:S(2)}) copy-start(f32[3,128]{1,0:T(4,128)} %param.31) | copy-start | bytes 4612
  124.2 191.8 %copy-start.2 = (f32[2,4096]{1,0:T(2,128)S(1)}, f32[2,4096]{1,0:T(2,128)}, u32[]{:S(2)}) copy-start(f32[2,4096]{1,0:T(2,128)} %param.35) | copy-start | bytes 98308
  267.4 49.2 %copy-start.10 = (f32[5,128]{1,0:T(8,128)}, f32[5,128]{1,0:T(8,128)S(1)}, u32[]{:S(2)}) copy-start(f32[5,128]{1,0:T(8,128)S(1)} %get-tuple-element.51) | copy-start | bytes 7684
  268.1 48.5 %copy-start.3 = (f32[2,4096]{1,0:T(2,128)}, f32[2,4096]{1,0:T(2,128)S(1)}, u32[]{:S(2)}) copy-start(f32[2,4096]{1,0:T(2,128)S(1)} %get-tuple-element.47) | copy-start | bytes 98308
  269.6 47.1 %copy-start.13 = (f32[3,128]{1,0:T(4,128)}, f32[3,128]{1,0:T(4,128)S(1)}, u32[]{:S(2)}) copy-start(f32[3,128]{1,0:T(4,128)S(1)} %get-tuple-element.49) | copy-start | bytes 4612
Sparse Core Ops, SparseCore 0:
  140.1 123.1 all-reduce.7
where the time goes:
time: 324 us
  waiting for transfers between devices  123 us (38%)
  local copies, waits for them, and re-layouts  73.3 us (23%)
  blocking collectives  50.1 us (15%)
  matrix products  25.8 us (8%)
  other arithmetic  25.7 us (8%)
  between operations  21.7 us (7%)
  starting transfers between devices  3.56 us (1%)
    psum x1, waiting for transfers between devices, local(): summed = lax.psum(packed, ('tm', 'cal'))  123 us
    psum x1, blocking collectives, local(): lax.psum(jnp.zeros((1, lane), jnp.float32).at[0, 0].set(next_local), ('tm...  42.5 us
    eq x1, local copies, waits for them, and re-layouts, local(): knot_hot = (local_knot[None] == knot_iota).astype(jnp.float32)  38.5 us
    eq x1, local copies, waits for them, and re-layouts, local(): high[None] == lax.broadcasted_iota(jnp.int32, (rows, 1, 1), 0)  20.5 us
    dot_general x1, matrix products, local(): jnp.einsum('hso,lso->hl', high_hot, cal_weighted, precision=EXACT)  11.2 us
    mul x1, local copies, waits for them, and re-layouts, local(): cal_weighted = (cal_design * weighted)[None] * low_hot  9.32 us
    dot_general x1, matrix products, local(): row_vals = jnp.einsum('hl,hso->lso', cal_table, high_hot, precision=EXACT)  8.23 us
    all_gather x1, blocking collectives, local(): cal_values = lax.all_gather(cal_dir, 'cal', axis=0, tiled=True)  7.65 us
  transfers between devices with their start and end apart: 3, of which 1 were waited for; matrix products, arithmetic and copies ran while one was open for 34% of the time, Pallas kernels for 0%

commit v1 on v0

--- a/solution.py
+++ b/solution.py
@@ -48,7 +48,12 @@
     rows = cal_size // lane
     src_rows, slots = obs_phase.shape
     first_row = (lax.axis_index("tm") == 0).astype(jnp.float32)
-    cal_values = lax.all_gather(cal_dir, "cal", axis=0, tiled=True)
+    ring = [cal_dir]
+    for hop in range(3):
+        ring.append(lax.ppermute(ring[-1], "cal", [(dev, (dev + 1) % 4) for dev in range(4)]))
+    cal_values = jnp.roll(
+        jnp.concatenate(ring[::-1], axis=0), (lax.axis_index("cal") + 1) * ring[0].shape[0], axis=0
+    )
     edge_knots = passed_along(att_dir[:, :3], ("tm", "cal"), -1)
     att_ext = jnp.concatenate([att_dir, edge_knots], axis=1)
     live_mask = (lax.broadcasted_iota(jnp.int32, obs_phase.shape, 1) < obs_count[:, None]).astype(

time: 324 us -> 323 us (level)
  blocking collectives: 50.1 us -> 42.5 us
  starting transfers between devices: 3.56 us -> 7.34 us
    all_gather x1 -> x0, blocking collectives: 7.65 us -> none  [local(): cal_values = lax.all_gather(cal_dir, 'cal', axis=0, tiled=True)]
    ppermute x0 -> x3, starting transfers between devices: none -> 4.51 us  [local(): lax.ppermute(ring[-1], 'cal', [(dev, (dev + 1) % 4) for dev in range(4)])]
  transfers between devices with their start and end apart: 3 -> 6, of which waited for: 1 -> 2; matrix products, arithmetic and copies ran while one was open for 34% -> 32% of each run, Pallas kernels for 0% -> 0%
where the time goes in v1:
time: 323 us; the launch traced here: 322 us
  waiting for transfers between devices  126 us (39%)
  local copies, waits for them, and re-layouts  73.5 us (23%)
  blocking collectives  42.5 us (13%)
  other arithmetic  25.7 us (8%)
  matrix products  25.5 us (8%)
  between operations  21.7 us (7%)
  starting transfers between devices  7.34 us (2%)
    psum x1, waiting for transfers between devices, local(): summed = lax.psum(packed, ('tm', 'cal'))  124 us
    psum x1, blocking collectives, local(): lax.psum(jnp.zeros((1, lane), jnp.float32).at[0, 0].set(next_local), ('tm...  42.5 us
    eq x1, local copies, waits for them, and re-layouts, local(): knot_hot = (local_knot[None] == knot_iota).astype(jnp.float32)  38.6 us
    eq x1, local copies, waits for them, and re-layouts, local(): high[None] == lax.broadcasted_iota(jnp.int32, (rows, 1, 1), 0)  20.5 us
    dot_general x1, matrix products, local(): jnp.einsum('hso,lso->hl', high_hot, cal_weighted, precision=EXACT)  11.1 us
    mul x1, local copies, waits for them, and re-layouts, local(): cal_weighted = (cal_design * weighted)[None] * low_hot  9.32 us
    dot_general x1, matrix products, local(): row_vals = jnp.einsum('hl,hso->lso', cal_table, high_hot, precision=EXACT)  8.26 us
  transfers between devices with their start and end apart: 6, of which 2 were waited for; matrix products, arithmetic and copies ran while one was open for 32% of the time, Pallas kernels for 0%

profile of v1, /device:TPU:0, one launch (start us, length us, event | category | flops | bytes accessed | tf_op | source)
XLA Modules:
  0.0 322.1 jit_solution(10112204643191235756)
XLA Ops:
  7.2 1.3 collective-permute-start
  8.5 1.2 collective-permute-start.1
  11.7 1.4 multiply_reduce_fusion.4
  13.0 1.3 multiply_reduce_fusion.8
  14.3 1.3 multiply_reduce_fusion.6
  19.8 0.9 add_select_fusion.1
  20.8 1.3 iota_compare_fusion.1
  22.2 38.6 %copy.35 = pred[128,128,128]{2,0,1:T(32,128)(4,1)S(1)} copy(pred[128,128,128]{1,0,2:T(32,128)(4,1)S(1)} %iota_compare_fusion.1) | data formatting | bytes 4194304 | tf_op jit(solution)/shard_map/eq | solution.py:65
  60.7 2.7 iota_compare_fusion
  63.5 20.5 %copy.41 = pred[256,128,128]{2,0,1:T(32,128)(4,1)} copy(pred[256,128,128]{1,0,2:T(32,128)(4,1)S(1)} %iota_compare_fusion) | data formatting | bytes 8388608 | tf_op jit(solution)/shard_map/eq | solution.py:77
  84.3 2.8 collective-permute-start.2
  87.1 2.1 fusion.28
  90.6 2.0 collective-permute-done.3
  93.0 8.3 %select_reduce_fusion = f32[128,128]{1,0:T(8,128)S(1)} fusion(s32[128,128]{1,0:T(8,128)S(1)} %get-tuple-element.62, pred[256,128,128]{2,0,1:T(32,128)(4,1)} %copy.41, f32[256,128]{1,0:T(8,128)S(1)} %reshape.140), kind=kOutput, calls=%fused_computation.1 | convolution fusion | flops 6448726016 | bytes 4456448 | tf_op jit(solution)/shard_map/hl,hso->lso/dot_general | solution.py:80
  102.0 4.0 %fusion.3 = f32[128,4,3]{0,1,2:T(4,128)S(1)} fusion(f32[4,3,128,128]{3,0,2,1:T(4,128)S(1)} %copy.44, s32[128,128]{0,1:T(8,128)S(1)} %copy.34), kind=kOutput, calls=%fused_computation.8 | convolution fusion | flops 304087040 | bytes 858112 | tf_op jit(solution)/shard_map/qso,jso->jq/dot_general | solution.py:96
  106.8 1.5 collective-permute-start.4
  108.3 4.7 %fusion = f32[128,128,128]{2,0,1:T(8,128)} fusion(f32[128,128]{1,0:T(8,128)S(1)} %get-tuple-element.52, s32[128,128]{1,0:T(8,128)S(1)} %get-tuple-element.62), kind=kLoop, calls=%fused_computation.4 | loop fusion | flops 4194304 | bytes 8519680 | tf_op jit(solution)/shard_map/mul | solution.py:104
  113.0 9.3 %copy.42 = f32[128,128,128]{1,0,2:T(8,128)} copy(f32[128,128,128]{2,0,1:T(8,128)} %fusion) | data formatting | bytes 16777216 | tf_op jit(solution)/shard_map/mul | solution.py:104
  122.3 11.1 %convolution_bitcast_fusion = f32[256,128]{1,0:T(8,128)S(1)} fusion(f32[128,128,128]{1,0,2:T(8,128)} %copy.42, s32[128,128]{0,1:T(8,128)S(1)} %copy.33), kind=kOutput, calls=%fused_computation.7 | convolution fusion | flops 6446645248 | bytes 8585216 | tf_op jit(solution)/shard_map/hso,lso->hl/dot_general | solution.py:105
  133.5 2.5 fusion.27
  136.0 1.4 scatter.11
  138.1 123.8 %all-reduce.8.cloned.1.call-done = f32[257,128]{1,0:T(8,128)} async-done(((f32[257,128]{1,0:T(8,128)}), f32[257,128]{1,0:T(8,128)}) %all-reduce.8.cloned.1.call-update) | async-done | bytes 131600 | tf_op jit(solution)/shard_map/psum | solution.py:108
  261.9 1.3 fusion.25
  270.2 42.5 %psum.15 = f32[1,128]{1,0:T(1,128)S(1)} all-reduce(f32[1,128]{1,0:T(1,128)S(1)} %scatter.14), channel_id=1, replica_groups=mesh['tm'=8,'cal'=4] {'tm','cal'}, use_global_device_ids=true, to_apply=%region_17.18 | all-reduce | flops 128 | bytes 1024 | tf_op jit(solution)/shard_map/psum | solution.py:124
  (78 shorter events, 12.5 us)
Async XLA Ops:
  7.2 254.7 %all-reduce.8.cloned.1.call-start = ((), (), s32[]{:S(2)}) async-start(), calls=%async_computation | async-start | bytes 270336 | tf_op jit(solution)/shard_map/psum | solution.py:108
  7.2 77.0 %collective-permute-start = (f32[3,3]{1,0:T(4,128)}, f32[3,3]{1,0:T(4,128)S(1)}, u32[]{:S(2)}, u32[]{:S(2)}) collective-permute-start(f32[3,3]{1,0:T(4,128)} %bitcast.73), channel_id=1, source_target_pairs={{1,0},{2,1},{3,2},{4,3},{5,4},{6,5},{7,6},{8,7},{9,8},{10,9},{11,1... | collective-permute-start | bytes 116 | tf_op jit(solution)/shard_map/ppermute | solution.py:12
  8.5 75.8 %collective-permute-start.1 = (f32[2,4096]{1,0:T(2,128)}, f32[2,4096]{1,0:T(2,128)S(1)}, u32[]{:S(2)}, u32[]{:S(2)}) collective-permute-start(f32[2,4096]{1,0:T(2,128)} %param.35), channel_id=1, source_target_pairs={{0,1},{1,2},{2,3},{3,0},{4,5},{5,6},{6,7},{7,4},{8,9},{9,10},{10,1... | collective-permute-start | bytes 98312 | tf_op jit(solution)/shard_map/ppermute | solution.py:53
  63.4 20.6 %copy-start = (f32[5,128,128]{2,1,0:T(8,128)S(1)}, f32[5,128,128]{2,1,0:T(8,128)}, u32[]{:S(2)}) copy-start(f32[5,128,128]{2,1,0:T(8,128)} %param.21) | copy-start | bytes 983044
  63.4 20.6 %copy-start.9 = (f32[5,128]{1,0:T(8,128)S(1)}, f32[5,128]{1,0:T(8,128)}, u32[]{:S(2)}) copy-start(f32[5,128]{1,0:T(8,128)} %param.33) | copy-start | bytes 7684
  63.4 20.8 %copy-start.8 = (f32[3,128]{1,0:T(4,128)S(1)}, f32[3,128]{1,0:T(4,128)}, u32[]{:S(2)}) copy-start(f32[3,128]{1,0:T(4,128)} %param.34) | copy-start | bytes 4612
  63.4 26.3 %copy-start.1 = (f32[3,128,128]{2,1,0:T(8,128)S(1)}, f32[3,128,128]{2,1,0:T(8,128)}, u32[]{:S(2)}) copy-start(f32[3,128,128]{2,1,0:T(8,128)} %param.22) | copy-start | bytes 589828
  84.0 8.6 %copy-start.2 = (f32[2,4096]{1,0:T(2,128)S(1)}, f32[2,4096]{1,0:T(2,128)}, u32[]{:S(2)}) copy-start(f32[2,4096]{1,0:T(2,128)} %param.35) | copy-start | bytes 98308
  84.3 4.9 %collective-permute-start.2 = (f32[2,4096]{1,0:T(2,128)S(1)}, f32[2,4096]{1,0:T(2,128)S(1)}, u32[]{:S(2)}, u32[]{:S(2)}) collective-permute-start(f32[2,4096]{1,0:T(2,128)S(1)} %collective-permute-done.1), channel_id=1, source_target_pairs={{0,1},{1,2},{2,3},{3,0},{4,5},{5,6},{6,7},{7,4},{8,9},{9,10},{10,1... | collective-permute-start | bytes 98312 | tf_op jit(solution)/shard_map/ppermute | solution.py:53
  89.2 3.4 %collective-permute-start.3 = (f32[2,4096]{1,0:T(2,128)S(1)}, f32[2,4096]{1,0:T(2,128)S(1)}, u32[]{:S(2)}, u32[]{:S(2)}) collective-permute-start(f32[2,4096]{1,0:T(2,128)S(1)} %collective-permute-done.2), channel_id=1, source_target_pairs={{0,1},{1,2},{2,3},{3,0},{4,5},{5,6},{6,7},{7,4},{8,9},{9,10},{10,1... | collective-permute-start | bytes 98312 | tf_op jit(solution)/shard_map/ppermute | solution.py:53
  92.9 8.3 %copy-start.5 = (f32[128,128]{1,0:T(8,128)S(1)}, f32[128,128]{1,0:T(8,128)}, u32[]{:S(2)}) copy-start(f32[128,128]{1,0:T(8,128)} %param.24) | copy-start | bytes 196612
  92.9 8.3 %copy-start.6 = (f32[128,128]{1,0:T(8,128)S(1)}, f32[128,128]{1,0:T(8,128)}, u32[]{:S(2)}) copy-start(f32[128,128]{1,0:T(8,128)} %param.25) | copy-start | bytes 196612
  92.9 8.3 %copy-start.7 = (f32[128,128]{1,0:T(8,128)S(1)}, f32[128,128]{1,0:T(8,128)}, u32[]{:S(2)}) copy-start(f32[128,128]{1,0:T(8,128)} %param.23) | copy-start | bytes 196612
  92.9 8.3 %copy-start.14 = (s32[128]{0:T(128)S(1)}, s32[128]{0:T(128)}, u32[]{:S(2)}) copy-start(s32[128]{0:T(128)} %param.29) | copy-start | bytes 1540
  106.8 31.3 %collective-permute-start.4 = (f32[3,3]{1,0:T(4,128)S(1)}, f32[3,3]{1,0:T(4,128)S(1)}, u32[]{:S(2)}, u32[]{:S(2)}) collective-permute-start(f32[3,3]{1,0:T(4,128)S(1)} %slice.142), channel_id=1, source_target_pairs={{0,1},{1,2},{2,3},{3,4},{4,5},{5,6},{6,7},{7,8},{8,9},{9,10},{10,1... | collective-permute-start | bytes 116 | tf_op jit(solution)/shard_map/ppermute | solution.py:12
  122.3 143.1 %copy-start.11 = (f32[5,128]{1,0:T(8,128)S(1)}, f32[5,128]{1,0:T(8,128)}, u32[]{:S(2)}) copy-start(f32[5,128]{1,0:T(8,128)} %param.30) | copy-start | bytes 7684
  122.3 143.7 %copy-start.4 = (f32[2,4096]{1,0:T(2,128)S(1)}, f32[2,4096]{1,0:T(2,128)}, u32[]{:S(2)}) copy-start(f32[2,4096]{1,0:T(2,128)} %param.32) | copy-start | bytes 98308
  122.3 145.1 %copy-start.12 = (f32[3,128]{1,0:T(4,128)S(1)}, f32[3,128]{1,0:T(4,128)}, u32[]{:S(2)}) copy-start(f32[3,128]{1,0:T(4,128)} %param.31) | copy-start | bytes 4612
  266.0 49.2 %copy-start.10 = (f32[5,128]{1,0:T(8,128)}, f32[5,128]{1,0:T(8,128)S(1)}, u32[]{:S(2)}) copy-start(f32[5,128]{1,0:T(8,128)S(1)} %get-tuple-element.51) | copy-start | bytes 7684
  266.7 48.5 %copy-start.3 = (f32[2,4096]{1,0:T(2,128)}, f32[2,4096]{1,0:T(2,128)S(1)}, u32[]{:S(2)}) copy-start(f32[2,4096]{1,0:T(2,128)S(1)} %get-tuple-element.47) | copy-start | bytes 98308
  268.2 47.1 %copy-start.13 = (f32[3,128]{1,0:T(4,128)}, f32[3,128]{1,0:T(4,128)S(1)}, u32[]{:S(2)}) copy-start(f32[3,128]{1,0:T(4,128)S(1)} %get-tuple-element.49) | copy-start | bytes 4612
Sparse Core Ops, SparseCore 0:
  138.2 123.6 all-reduce.7
